TPU v7x, 32 devices: a whole 2x2x4 slice. The times are simulated.
32 devices in a mesh: tile: 8 (over z, core), deg: 4 (over y, x).
Axes of the slice: x: 2, y: 2, z: 4, core: 2. Of those that a mesh axis runs over, the one named last changes fastest.
Arguments:
- field: float32 [3, 8, 128, 512], P(None, None, 'tile', 'deg'), may hold values from -6 to 6
- flow: float32 [3, 8, 128, 512], P(None, None, 'tile', 'deg'), may hold values from -3 to 3
- match_ops: bfloat16 [32, 512, 512], P(('tile', 'deg')), may hold values from -0.5 to 20.5
- wave_of_slot: int32 [32], replicated, may hold values from 0 to 31, each once
Outputs:
- advanced: float32 [3, 8, 128, 512], P(None, None, 'tile', 'deg')
Inputs may be any that keep to these rules, and one draw needn't show every extreme that they name: `wave_of_slot`: every wavenumber from 0 to 31 is named by exactly one slot.
All inputs are finite; a program needn't handle non-finite values.
Results may differ from a plain program's by a relative error of at most 0.00065.
Values may be sent and summed in bfloat16 or wider, within the bound.
No kernel may reach another device: no remote copies, remote signals or barrier semaphores. Data moves between devices by JAX's collectives and lax.ppermute only.
A program may use at most 64 MiB of HBM per device.

v0:
```python
import math
import jax
import jax.numpy as jnp
from jax import lax
from jax.sharding import PartitionSpec as P

P_SIZE = 8
diffusivity = 0.05
time_step = 0.01
highest = lax.Precision.HIGHEST
gll_interior = [0.2092992179024789, 0.5917001814331423, 0.8717401485096066]


def padded_2(value, sides, width):
    for axis, dim in sides:
        size, length = (lax.axis_size(axis), value.shape[dim])
        up = [(i, (i + 1) % size) for i in range(size)]
        down = [(j, i) for i, j in up]
        last = lax.slice_in_dim(value, length - width, length, axis=dim)
        first = lax.slice_in_dim(value, 0, width, axis=dim)
        before = lax.ppermute(last, axis, up)
        after = lax.ppermute(first, axis, down)
        value = jnp.concatenate([before, value, after], axis=dim)
    return value


def legendre_value(point, degree):
    previous = 1.0
    current = point
    for order in range(1, degree):
        following = ((2 * order + 1) * point * current - order * previous) / (order + 1)
        previous = current
        current = following
    return current


def gll_tables(count):
    degree = count - 1
    points = [-1.0] + [-value for value in reversed(gll_interior)] + list(gll_interior) + [1.0]
    values = [legendre_value(point, degree) for point in points]
    weights = [2.0 / (degree * (degree + 1) * value * value) for value in values]
    matrix = [
        [
            values[row] / (values[col] * (points[row] - points[col])) if row != col else 0.0
            for col in range(count)
        ]
        for row in range(count)
    ]
    matrix[0][0] = -degree * (degree + 1) / 4.0
    matrix[count - 1][count - 1] = degree * (degree + 1) / 4.0
    return (points, weights, matrix)


def apply_along(values, axis_pos, matrix):
    shape = values.shape
    blocks = values.reshape(
        shape[:axis_pos] + (shape[axis_pos] // P_SIZE, P_SIZE) + shape[axis_pos + 1 :]
    )
    letters = list("abcdefg"[: blocks.ndim])
    source = list(letters)
    source[axis_pos + 1] = "p"
    target = list(letters)
    target[axis_pos + 1] = "q"
    formula = "".join(source) + ",qp->" + "".join(target)
    return jnp.einsum(formula, blocks, matrix, precision=highest).reshape(shape)


def assemble_dim(values, axis_pos, left, right):
    shape = values.shape
    count = shape[axis_pos] // P_SIZE
    blocks = values.reshape(shape[:axis_pos] + (count, P_SIZE) + shape[axis_pos + 1 :])
    edge_shape = shape[:axis_pos] + (1, 1) + shape[axis_pos + 1 :]
    first = lax.slice_in_dim(blocks, 0, 1, axis=axis_pos + 1)
    last = lax.slice_in_dim(blocks, P_SIZE - 1, P_SIZE, axis=axis_pos + 1)
    before = jnp.concatenate(
        [left.reshape(edge_shape), lax.slice_in_dim(last, 0, count - 1, axis=axis_pos)],
        axis=axis_pos,
    )
    after = jnp.concatenate(
        [lax.slice_in_dim(first, 1, count, axis=axis_pos), right.reshape(edge_shape)], axis=axis_pos
    )
    middle = lax.slice_in_dim(blocks, 1, P_SIZE - 1, axis=axis_pos + 1)
    joined = jnp.concatenate([first + before, middle, last + after], axis=axis_pos + 1)
    return joined.reshape(shape)


def assembled_weights(weights, count, lead, trail):
    position = jnp.arange(count * P_SIZE, dtype=jnp.int32)
    local_point = position % P_SIZE
    element = position // P_SIZE
    base = jnp.tile(weights, count)
    starts = (
        jnp.where(local_point == 0, jnp.where(element > 0, 1.0, lead), 0.0) * weights[P_SIZE - 1]
    )
    ends = (
        jnp.where(local_point == P_SIZE - 1, jnp.where(element < count - 1, 1.0, trail), 0.0)
        * weights[0]
    )
    return base + starts + ends


def phases(waves, elem_start, elem_count, span, points):
    element = elem_start + jnp.arange(elem_count * P_SIZE, dtype=jnp.int32) // P_SIZE
    whole = waves[:, None] * (2 * element + 1)[None, :] % span
    fraction = waves.astype(jnp.float32)[:, None] * jnp.tile(points, elem_count)[None, :]
    return 2.0 * math.pi / span * (whole.astype(jnp.float32) + fraction)


def local(field, flow, match_ops, wave_of_slot):
    tiles = lax.axis_size("tile")
    groups = lax.axis_size("deg")
    tile_index = lax.axis_index("tile")
    group_index = lax.axis_index("deg")
    radial_nodes = field.shape[1]
    na_dev = field.shape[2]
    nb_dev = field.shape[3]
    elems_a = na_dev // P_SIZE
    elems_b = nb_dev // P_SIZE
    span = 2 * elems_a * tiles
    per_tile = wave_of_slot.shape[0] // tiles
    scale = P_SIZE / (na_dev * tiles)
    points_list, weights_list, matrix_list = gll_tables(P_SIZE)
    points = jnp.asarray(points_list, jnp.float32)
    weights = jnp.asarray(weights_list, jnp.float32)
    dmat = jnp.asarray(matrix_list, jnp.float32)
    block = jnp.kron(jnp.eye(elems_b, dtype=jnp.float32), dmat)
    lead = (group_index > 0).astype(jnp.float32)
    trail = (group_index < groups - 1).astype(jnp.float32)
    w_r = jnp.tile(weights, radial_nodes // P_SIZE)
    w_a = jnp.tile(weights, elems_a)
    w_b = jnp.tile(weights, elems_b)
    mass3 = w_r[:, None, None] * w_a[None, :, None] * w_b[None, None, :]
    surface_weight = w_a[:, None] * w_b[None, :]
    assembled = (
        assembled_weights(weights, radial_nodes // P_SIZE, 0.0, 0.0)[:, None, None]
        * assembled_weights(weights, elems_a, 1.0, 1.0)[None, :, None]
        * assembled_weights(weights, elems_b, lead, trail)[None, None, :]
    )
    column_mask = jnp.concatenate([lead[None], jnp.ones((nb_dev,), jnp.float32), trail[None]])

    def derive(values, direction, transpose):
        if direction == 2:
            table = block if transpose else block.T
            return jnp.dot(values, table, precision=highest)
        return apply_along(values, direction, dmat.T if transpose else dmat)

    flow_parts = [flow[0], flow[1], flow[2]]
    grad_flow = [
        [derive(flow_parts[component], direction, False) for direction in range(3)]
        for component in range(3)
    ]

    def analyse(surface):
        angle = phases(wave_of_slot, tile_index * elems_a, elems_a, span, points)
        table = (
            jnp.stack([jnp.cos(angle), jnp.sin(angle)], axis=1) * (w_a * scale)[None, None, :]
        ).reshape(lax.axis_size("tile") * per_tile * 2, na_dev)
        return jnp.dot(table, surface, precision=highest).reshape(
            lax.axis_size("tile") * per_tile, 2, nb_dev
        )

    def surface_flux(surface):
        coeff = lax.psum_scatter(analyse(surface), "tile", scatter_dimension=0, tiled=True)
        owned = lax.all_to_all(
            coeff.astype(jnp.bfloat16), "deg", split_axis=0, concat_axis=2, tiled=True
        )
        mapped = jnp.einsum("kpq,kcq->kcp", match_ops, owned, preferred_element_type=jnp.float32)
        matched = lax.all_to_all(mapped, "deg", split_axis=2, concat_axis=0, tiled=True)
        my_waves = lax.dynamic_slice_in_dim(wave_of_slot, tile_index * per_tile, per_tile)
        flat_matched = matched.reshape(per_tile * 2, nb_dev)
        angle = phases(
            my_waves, jnp.int32(0) // P_SIZE, lax.axis_size("tile") * na_dev // P_SIZE, span, points
        )
        table = jnp.stack([jnp.cos(angle).T, jnp.sin(angle).T], axis=2).reshape(
            lax.axis_size("tile") * na_dev, per_tile * 2
        )
        total = lax.psum_scatter(
            jnp.dot(table, flat_matched, precision=highest), "tile", scatter_dimension=0, tiled=True
        )
        return -total

    def tendency(parts):
        rhs = []
        for component in range(3):
            slopes = [derive(parts[component], direction, False) for direction in range(3)]
            stretch = (
                parts[0] * grad_flow[component][0]
                + parts[1] * grad_flow[component][1]
                + parts[2] * grad_flow[component][2]
            )
            carried = (
                flow_parts[0] * slopes[0] + flow_parts[1] * slopes[1] + flow_parts[2] * slopes[2]
            )
            spread = (
                derive(mass3 * slopes[0], 0, True)
                + derive(mass3 * slopes[1], 1, True)
                + derive(mass3 * slopes[2], 2, True)
            )
            rhs.append(mass3 * (stretch - carried) - diffusivity * spread)
        flux = surface_flux(parts[0][radial_nodes - 1])
        rhs[0] = rhs[0].at[radial_nodes - 1].add(diffusivity * surface_weight * flux)
        stacked = jnp.stack(rhs)
        plane_r = jnp.zeros_like(lax.slice_in_dim(stacked, 0, 1, axis=1))
        stacked = assemble_dim(stacked, 1, plane_r, plane_r)
        padded = padded_2(stacked.astype(jnp.bfloat16), (("tile", 2), ("deg", 3)), 1).astype(
            stacked.dtype
        )
        padded = padded * column_mask
        along_a = assemble_dim(padded[:, :, 1:-1, :], 2, padded[:, :, 0:1, :], padded[:, :, -1:, :])
        along_b = assemble_dim(
            along_a[:, :, :, 1:-1], 3, along_a[:, :, :, 0:1], along_a[:, :, :, -1:]
        )
        return along_b / assembled[None]

    section = field + time_step * tendency([field[0], field[1], field[2]])
    return 0.5 * (field + section + time_step * tendency([section[0], section[1], section[2]]))


def solution(mesh):
    placed = (
        P(None, None, "tile", "deg"),
        P(None, None, "tile", "deg"),
        P(("tile", "deg"), None, None),
        P(),
    )
    return jax.shard_map(
        local, mesh=mesh, in_specs=placed, out_specs=P(None, None, "tile", "deg"), check_vma=False
    )
```

profile of v0, /device:TPU:0, one launch (start us, length us, event | category | flops | bytes accessed | tf_op | source)
XLA Modules:
  0.0 227.2 jit_solution(8538211180107501560)
XLA Ops:
  10.2 1.0 fusion.116
  11.2 30.3 %all-reduce = bf16[32,2,128]{2,0,1:T(8,128)(2,1)S(1)} all-reduce(f32[32,2,128]{2,0,1:T(8,128)S(1)} %fusion.116), channel_id=2, replica_groups=mesh['tile'=8,'deg'=4] {'tile'}, use_global_device_ids=true, to_apply=%region_0.1.clone | all-reduce | flops 8192 | bytes 49152
  41.5 1.2 dynamic-slice.16
  43.9 3.7 %all-to-all-start = ((bf16[4,2,128]{2,1,0:T(2,128)(2,1)}), bf16[4,2,128]{2,1,0:T(2,128)(2,1)S(1)}, u32[]{:S(2)}, u32[]{:S(2)}) async-start(bf16[4,2,128]{2,1,0:T(2,128)(2,1)} %copy.334), calls=%async_computation | async-start | bytes 4096 | tf_op jit(solution)/shard_map/all_to_all | solution.py:164
  49.4 1.1 fusion.51
  50.5 1.0 convolution_bitcast_fusion.6
  51.6 0.9 fusion.169
  53.3 1.0 fusion.54
  62.6 1.2 reduce.4
  64.6 4.2 %all-to-all-start.1 = ((f32[4,1,256]{2,1,0:T(1,128)}), f32[4,1,256]{2,1,0:T(1,128)S(1)}, u32[]{:S(2)}, u32[]{:S(2)}) async-start(f32[4,1,256]{2,1,0:T(1,128)} %reshape.1012), calls=%async_computation.1 | async-start | bytes 8192 | tf_op jit(solution)/shard_map/all_to_all | solution.py:168
  68.8 4.7 %all-to-all-done.1 = f32[4,1,256]{2,1,0:T(1,128)S(1)} async-done(((f32[4,1,256]{2,1,0:T(1,128)}), f32[4,1,256]{2,1,0:T(1,128)S(1)}, u32[]{:S(2)}, u32[]{:S(2)}) %all-to-all-start.1) | async-done | bytes 4128 | tf_op jit(solution)/shard_map/all_to_all | solution.py:168
  76.1 25.9 %reduce-scatter.5.cloned.1.call-done = f32[16,128]{1,0:T(8,128)} async-done(((f32[128,128]{1,0:T(8,128)}), f32[16,128]{1,0:T(8,128)}) %reduce-scatter.5.cloned.1.call-update) | async-done | bytes 8208 | tf_op jit(solution)/shard_map/reduce_scatter | solution.py:177
  104.4 3.5 %collective-permute-done = bf16[3,8,1,128]{3,1,2,0:T(8,128)(2,1)S(1)} collective-permute-done((bf16[3,8,1,128]{3,1,2,0:T(8,128)(2,1)S(1)}, bf16[3,8,1,128]{3,1,2,0:T(8,128)(2,1)S(1)}, u32[]{:S(2)}, u32[]{:S(2)}) %collective-permute-start) | collective-permute-done | bytes 6176 | tf_op jit(solution)/shard_map/ppermute | solution.py:21
  108.0 2.7 %collective-permute-start.3 = (bf16[3,8,18,1]{3,1,2,0:T(8,128)(2,1)S(1)}, bf16[3,8,18,1]{3,1,2,0:T(8,128)(2,1)S(1)}, u32[]{:S(2)}, u32[]{:S(2)}) collective-permute-start(bf16[3,8,18,1]{3,1,2,0:T(8,128)(2,1)S(1)} %get-tuple-element.73), channel_id=1, source_target_pairs={{1,0},{2,1},{3,2},{0,3},{5,4},{6,5},{7,6},{4,7},{9,8},{10,9},{11,1... | collective-permute-start | bytes 2600 | tf_op jit(solution)/shard_map/ppermute | solution.py:22
  110.8 2.2 collective-permute-done.3
  113.0 3.3 %collective-permute-done.2 = bf16[3,8,18,1]{3,1,2,0:T(8,128)(2,1)S(1)} collective-permute-done((bf16[3,8,18,1]{3,1,2,0:T(8,128)(2,1)S(1)}, bf16[3,8,18,1]{3,1,2,0:T(8,128)(2,1)S(1)}, u32[]{:S(2)}, u32[]{:S(2)}) %collective-permute-start.2) | collective-permute-done | bytes 896 | tf_op jit(solution)/shard_map/ppermute | solution.py:21
  117.7 1.3 slice.297
  120.0 2.0 maximum_bitcast_fusion
  126.1 26.0 %all-reduce.1 = bf16[32,2,128]{2,0,1:T(8,128)(2,1)S(1)} all-reduce(f32[32,2,128]{2,0,1:T(8,128)S(1)} %fusion.115), channel_id=4, replica_groups=mesh['tile'=8,'deg'=4] {'tile'}, use_global_device_ids=true, to_apply=%region_2.3.clone | all-reduce | flops 8192 | bytes 49152
  152.7 3.2 %all-to-all-start.2 = ((bf16[4,2,128]{2,1,0:T(2,128)(2,1)}), bf16[4,2,128]{2,1,0:T(2,128)(2,1)S(1)}, u32[]{:S(2)}, u32[]{:S(2)}) async-start(bf16[4,2,128]{2,1,0:T(2,128)(2,1)} %copy.387), calls=%async_computation.3 | async-start | bytes 4096 | tf_op jit(solution)/shard_map/all_to_all | solution.py:164
  156.9 3.5 %all-to-all-done.2 = bf16[4,2,128]{2,1,0:T(2,128)(2,1)S(1)} async-done(((bf16[4,2,128]{2,1,0:T(2,128)(2,1)}), bf16[4,2,128]{2,1,0:T(2,128)(2,1)S(1)}, u32[]{:S(2)}, u32[]{:S(2)}) %all-to-all-start.2) | async-done | bytes 2080 | tf_op jit(solution)/shard_map/all_to_all | solution.py:164
  160.7 1.2 reduce.6
  162.7 3.2 %all-to-all-start.3 = ((f32[4,1,256]{2,1,0:T(1,128)}), f32[4,1,256]{2,1,0:T(1,128)S(1)}, u32[]{:S(2)}, u32[]{:S(2)}) async-start(f32[4,1,256]{2,1,0:T(1,128)} %reshape.1014), calls=%async_computation.4 | async-start | bytes 8192 | tf_op jit(solution)/shard_map/all_to_all | solution.py:168
  166.3 4.3 %all-to-all-done.3 = f32[4,1,256]{2,1,0:T(1,128)S(1)} async-done(((f32[4,1,256]{2,1,0:T(1,128)}), f32[4,1,256]{2,1,0:T(1,128)S(1)}, u32[]{:S(2)}, u32[]{:S(2)}) %all-to-all-start.3) | async-done | bytes 4128 | tf_op jit(solution)/shard_map/all_to_all | solution.py:168
  172.9 26.3 %reduce-scatter.7.cloned.1.call-done = f32[16,128]{1,0:T(8,128)} async-done(((f32[128,128]{1,0:T(8,128)}), f32[16,128]{1,0:T(8,128)}) %reduce-scatter.7.cloned.1.call-update) | async-done | bytes 8208 | tf_op jit(solution)/shard_map/reduce_scatter | solution.py:177
  200.6 0.9 collective-permute-done.5
  201.6 3.5 %collective-permute-done.4 = bf16[3,8,1,128]{3,1,2,0:T(8,128)(2,1)S(1)} collective-permute-done((bf16[3,8,1,128]{3,1,2,0:T(8,128)(2,1)S(1)}, bf16[3,8,1,128]{3,1,2,0:T(8,128)(2,1)S(1)}, u32[]{:S(2)}, u32[]{:S(2)}) %collective-permute-start.4) | collective-permute-done | bytes 6176 | tf_op jit(solution)/shard_map/ppermute | solution.py:21
  205.2 2.7 %collective-permute-start.7 = (bf16[3,8,18,1]{3,1,2,0:T(8,128)(2,1)S(1)}, bf16[3,8,18,1]{3,1,2,0:T(8,128)(2,1)S(1)}, u32[]{:S(2)}, u32[]{:S(2)}) collective-permute-start(bf16[3,8,18,1]{3,1,2,0:T(8,128)(2,1)S(1)} %get-tuple-element.71), channel_id=1, source_target_pairs={{1,0},{2,1},{3,2},{0,3},{5,4},{6,5},{7,6},{4,7},{9,8},{10,9},{11,1... | collective-permute-start | bytes 2600 | tf_op jit(solution)/shard_map/ppermute | solution.py:22
  207.9 2.3 %collective-permute-done.7 = bf16[3,8,18,1]{3,1,2,0:T(8,128)(2,1)S(1)} collective-permute-done((bf16[3,8,18,1]{3,1,2,0:T(8,128)(2,1)S(1)}, bf16[3,8,18,1]{3,1,2,0:T(8,128)(2,1)S(1)}, u32[]{:S(2)}, u32[]{:S(2)}) %collective-permute-start.7) | collective-permute-done | bytes 896 | tf_op jit(solution)/shard_map/ppermute | solution.py:22
  210.2 3.3 %collective-permute-done.6 = bf16[3,8,18,1]{3,1,2,0:T(8,128)(2,1)S(1)} collective-permute-done((bf16[3,8,18,1]{3,1,2,0:T(8,128)(2,1)S(1)}, bf16[3,8,18,1]{3,1,2,0:T(8,128)(2,1)S(1)}, u32[]{:S(2)}, u32[]{:S(2)}) %collective-permute-start.6) | collective-permute-done | bytes 896 | tf_op jit(solution)/shard_map/ppermute | solution.py:21
  214.8 1.3 slice.320
  217.1 2.0 maximum_bitcast_fusion.1
  (224 shorter events, 36.4 us)
Async XLA Ops:
  6.5 55.3 %copy-start = (bf16[1,512,512]{2,1,0:T(8,128)(2,1)S(1)}, bf16[1,512,512]{2,1,0:T(8,128)(2,1)}, u32[]{:S(2)}) copy-start(bf16[1,512,512]{2,1,0:T(8,128)(2,1)} %param.13) | copy-start | bytes 1572868
  8.7 39.7 %copy-start.32 = (f32[16]{0:T(128)}, f32[16]{0:T(128)S(1)}, u32[]{:S(2)}) copy-start(f32[16]{0:T(128)S(1)} %get-tuple-element.95) | copy-start | bytes 196
  43.9 17.9 %all-to-all-start = ((bf16[4,2,128]{2,1,0:T(2,128)(2,1)}), bf16[4,2,128]{2,1,0:T(2,128)(2,1)S(1)}, u32[]{:S(2)}, u32[]{:S(2)}) async-start(bf16[4,2,128]{2,1,0:T(2,128)(2,1)} %copy.334), calls=%async_computation | async-start | bytes 4096 | tf_op jit(solution)/shard_map/all_to_all | solution.py:164
  48.5 12.3 %copy-start.24 = (f32[8,2,8]{2,1,0:T(2,128)}, f32[8,2,8]{2,1,0:T(2,128)S(1)}, u32[]{:S(2)}) copy-start(f32[8,2,8]{2,1,0:T(2,128)S(1)} %broadcast_multiply_fusion.3) | copy-start | bytes 1540
  49.4 6.3 %copy-start.2 = (f32[3,8,16,128]{3,2,1,0:T(8,128)S(1)}, f32[3,8,16,128]{3,2,1,0:T(8,128)}, u32[]{:S(2)}) copy-start(f32[3,8,16,128]{3,2,1,0:T(8,128)} %param.12) | copy-start | bytes 589828
  49.4 6.5 %copy-start.1 = (f32[3,8,16,128]{3,2,1,0:T(8,128)S(1)}, f32[3,8,16,128]{3,2,1,0:T(8,128)}, u32[]{:S(2)}) copy-start(f32[3,8,16,128]{3,2,1,0:T(8,128)} %param.11) | copy-start | bytes 589828
  51.6 7.2 %copy-start.10 = (f32[8,16,128]{2,1,0:T(8,128)}, f32[8,16,128]{2,1,0:T(8,128)S(1)}, u32[]{:S(2)}) copy-start(f32[8,16,128]{2,1,0:T(8,128)S(1)} %convolution_bitcast_fusion.6) | copy-start | bytes 196612
  51.6 4.9 %copy-start.22 = (f32[8,8,1,1]{1,0,3,2:T(8,128)S(1)}, f32[8,8,1,1]{1,0,3,2:T(8,128)}, u32[]{:S(2)}) copy-start(f32[8,8,1,1]{1,0,3,2:T(8,128)} %constant.239) | copy-start | bytes 772
  54.3 3.2 %copy-start.23 = (f32[8]{0:T(128)S(1)}, f32[8]{0:T(128)}, u32[]{:S(2)}) copy-start(f32[8]{0:T(128)} %constant.223.clone) | copy-start | bytes 100
  55.2 2.8 %copy-start.3 = (f32[8,8,1]{1,0,2:T(8,128)S(1)}, f32[8,8,1]{1,0,2:T(8,128)}, u32[]{:S(2)}) copy-start(f32[8,8,1]{1,0,2:T(8,128)} %constant.238) | copy-start | bytes 772
  56.0 3.1 %copy-start.4 = (f32[8,16,128]{2,1,0:T(8,128)}, f32[8,16,128]{2,1,0:T(8,128)S(1)}, u32[]{:S(2)}) copy-start(f32[8,16,128]{2,1,0:T(8,128)S(1)} %convolution_bitcast_fusion.5) | copy-start | bytes 196612
  56.5 19.0 %copy-start.6 = (f32[8,16,128]{2,1,0:T(8,128)}, f32[8,16,128]{2,1,0:T(8,128)S(1)}, u32[]{:S(2)}) copy-start(f32[8,16,128]{2,1,0:T(8,128)S(1)} %convolution_bitcast_fusion.9) | copy-start | bytes 196612
  57.0 3.0 %copy-start.31 = (f32[8]{0:T(128)S(1)}, f32[8]{0:T(128)}, u32[]{:S(2)}) copy-start(f32[8]{0:T(128)} %constant.222.clone) | copy-start | bytes 100
  57.0 3.1 %copy-start.30 = (s32[32]{0:T(128)S(1)}, s32[32]{0:T(128)}, u32[]{:S(2)}) copy-start(s32[32]{0:T(128)} %param.14) | copy-start | bytes 388
  57.3 4.0 %copy-start.8 = (f32[8,16,128]{2,1,0:T(8,128)}, f32[8,16,128]{2,1,0:T(8,128)S(1)}, u32[]{:S(2)}) copy-start(f32[8,16,128]{2,1,0:T(8,128)S(1)} %convolution_bitcast_fusion.13) | copy-start | bytes 196612
  57.5 3.8 %copy-start.12 = (f32[8,16,128]{2,1,0:T(8,128)}, f32[8,16,128]{2,1,0:T(8,128)S(1)}, u32[]{:S(2)}) copy-start(f32[8,16,128]{2,1,0:T(8,128)S(1)} %convolution_bitcast_fusion.14) | copy-start | bytes 196612
  58.4 2.7 %copy-start.14 = (f32[8,16,128]{2,0,1:T(8,128)}, f32[8,16,128]{2,0,1:T(8,128)S(1)}, u32[]{:S(2)}) copy-start(f32[8,16,128]{2,0,1:T(8,128)S(1)} %fusion.98) | copy-start | bytes 196612
  59.5 16.0 %copy-start.16 = (f32[8,16,128]{2,0,1:T(8,128)}, f32[8,16,128]{2,0,1:T(8,128)S(1)}, u32[]{:S(2)}) copy-start(f32[8,16,128]{2,0,1:T(8,128)S(1)} %fusion.84) | copy-start | bytes 196612
  61.8 14.1 %copy-start.20 = (f32[8,16,128]{2,1,0:T(8,128)}, f32[8,16,128]{2,1,0:T(8,128)S(1)}, u32[]{:S(2)}) copy-start(f32[8,16,128]{2,1,0:T(8,128)S(1)} %convolution_bitcast_fusion.10) | copy-start | bytes 196612
  64.6 8.9 %all-to-all-start.1 = ((f32[4,1,256]{2,1,0:T(1,128)}), f32[4,1,256]{2,1,0:T(1,128)S(1)}, u32[]{:S(2)}, u32[]{:S(2)}) async-start(f32[4,1,256]{2,1,0:T(1,128)} %reshape.1012), calls=%async_computation.1 | async-start | bytes 8192 | tf_op jit(solution)/shard_map/all_to_all | solution.py:168
  68.8 33.2 %reduce-scatter.5.cloned.1.call-start = ((), (), s32[]{:S(2)}) async-start(), calls=%async_computation.6 | async-start | bytes 73728 | tf_op jit(solution)/shard_map/reduce_scatter | solution.py:177
  102.8 1.5 collective-permute-start.1
  103.0 4.9 %collective-permute-start = (bf16[3,8,1,128]{3,1,2,0:T(8,128)(2,1)S(1)}, bf16[3,8,1,128]{3,1,2,0:T(8,128)(2,1)S(1)}, u32[]{:S(2)}, u32[]{:S(2)}) collective-permute-start(bf16[3,8,1,128]{3,1,2,0:T(8,128)(2,1)S(1)} %get-tuple-element.76), channel_id=1, source_target_pairs={{0,4},{4,8},{8,12},{12,16},{16,20},{20,24},{24,28},{28,0},{1,5},{5... | collective-permute-start | bytes 18440 | tf_op jit(solution)/shard_map/ppermute | solution.py:21
  108.0 5.0 %collective-permute-start.3 = (bf16[3,8,18,1]{3,1,2,0:T(8,128)(2,1)S(1)}, bf16[3,8,18,1]{3,1,2,0:T(8,128)(2,1)S(1)}, u32[]{:S(2)}, u32[]{:S(2)}) collective-permute-start(bf16[3,8,18,1]{3,1,2,0:T(8,128)(2,1)S(1)} %get-tuple-element.73), channel_id=1, source_target_pairs={{1,0},{2,1},{3,2},{0,3},{5,4},{6,5},{7,6},{4,7},{9,8},{10,9},{11,1... | collective-permute-start | bytes 2600 | tf_op jit(solution)/shard_map/ppermute | solution.py:22
  110.7 5.6 %collective-permute-start.2 = (bf16[3,8,18,1]{3,1,2,0:T(8,128)(2,1)S(1)}, bf16[3,8,18,1]{3,1,2,0:T(8,128)(2,1)S(1)}, u32[]{:S(2)}, u32[]{:S(2)}) collective-permute-start(bf16[3,8,18,1]{3,1,2,0:T(8,128)(2,1)S(1)} %get-tuple-element.72), channel_id=1, source_target_pairs={{0,1},{1,2},{2,3},{3,0},{4,5},{5,6},{6,7},{7,4},{8,9},{9,10},{10,1... | collective-permute-start | bytes 2600 | tf_op jit(solution)/shard_map/ppermute | solution.py:21
  152.7 7.8 %all-to-all-start.2 = ((bf16[4,2,128]{2,1,0:T(2,128)(2,1)}), bf16[4,2,128]{2,1,0:T(2,128)(2,1)S(1)}, u32[]{:S(2)}, u32[]{:S(2)}) async-start(bf16[4,2,128]{2,1,0:T(2,128)(2,1)} %copy.387), calls=%async_computation.3 | async-start | bytes 4096 | tf_op jit(solution)/shard_map/all_to_all | solution.py:164
  162.7 7.9 %all-to-all-start.3 = ((f32[4,1,256]{2,1,0:T(1,128)}), f32[4,1,256]{2,1,0:T(1,128)S(1)}, u32[]{:S(2)}, u32[]{:S(2)}) async-start(f32[4,1,256]{2,1,0:T(1,128)} %reshape.1014), calls=%async_computation.4 | async-start | bytes 8192 | tf_op jit(solution)/shard_map/all_to_all | solution.py:168
  166.0 33.2 %reduce-scatter.7.cloned.1.call-start = ((), (), s32[]{:S(2)}) async-start(), calls=%async_computation.7 | async-start | bytes 73728 | tf_op jit(solution)/shard_map/reduce_scatter | solution.py:177
  200.0 1.5 collective-permute-start.5
  200.2 4.9 %collective-permute-start.4 = (bf16[3,8,1,128]{3,1,2,0:T(8,128)(2,1)S(1)}, bf16[3,8,1,128]{3,1,2,0:T(8,128)(2,1)S(1)}, u32[]{:S(2)}, u32[]{:S(2)}) collective-permute-start(bf16[3,8,1,128]{3,1,2,0:T(8,128)(2,1)S(1)} %get-tuple-element.74), channel_id=1, source_target_pairs={{0,4},{4,8},{8,12},{12,16},{16,20},{20,24},{24,28},{28,0},{1,5},{5... | collective-permute-start | bytes 18440 | tf_op jit(solution)/shard_map/ppermute | solution.py:21
  205.2 5.0 %collective-permute-start.7 = (bf16[3,8,18,1]{3,1,2,0:T(8,128)(2,1)S(1)}, bf16[3,8,18,1]{3,1,2,0:T(8,128)(2,1)S(1)}, u32[]{:S(2)}, u32[]{:S(2)}) collective-permute-start(bf16[3,8,18,1]{3,1,2,0:T(8,128)(2,1)S(1)} %get-tuple-element.71), channel_id=1, source_target_pairs={{1,0},{2,1},{3,2},{0,3},{5,4},{6,5},{7,6},{4,7},{9,8},{10,9},{11,1... | collective-permute-start | bytes 2600 | tf_op jit(solution)/shard_map/ppermute | solution.py:22
  207.9 5.6 %collective-permute-start.6 = (bf16[3,8,18,1]{3,1,2,0:T(8,128)(2,1)S(1)}, bf16[3,8,18,1]{3,1,2,0:T(8,128)(2,1)S(1)}, u32[]{:S(2)}, u32[]{:S(2)}) collective-permute-start(bf16[3,8,18,1]{3,1,2,0:T(8,128)(2,1)S(1)} %get-tuple-element.70), channel_id=1, source_target_pairs={{0,1},{1,2},{2,3},{3,0},{4,5},{5,6},{6,7},{7,4},{8,9},{9,10},{10,1... | collective-permute-start | bytes 2600 | tf_op jit(solution)/shard_map/ppermute | solution.py:21
  (16 other events, 25.0 us)
Sparse Core Ops, SparseCore 0:
  75.7 26.3 reduce-scatter.4
  172.8 26.3 reduce-scatter.6
where the time goes:
time: 228 us; the launch traced here: 227 us
  waiting for transfers between devices  84.8 us (37%)
  blocking collectives  56.3 us (25%)
  starting transfers between devices  21 us (9%)
  local copies, waits for them, and re-layouts  17.1 us (8%)
  matrix products  16.9 us (7%)
  other arithmetic  15.9 us (7%)
  between operations  15.3 us (7%)
    unnamed x2, blocking collectives  56.3 us
    reduce_scatter x2, waiting for transfers between devices, surface_flux(): lax.psum_scatter(jnp.dot(table, flat_matched, precision=highest), 'tile',...  52.2 us
    ppermute x4, waiting for transfers between devices, padded_2(): before = lax.ppermute(last, axis, up)  13.6 us
    dot_general x30, matrix products, apply_along(): return jnp.einsum(formula, blocks, matrix, precision=highest).reshape(shape)  9.26 us
    all_to_all x2, waiting for transfers between devices, surface_flux(): lax.all_to_all(mapped, 'deg', split_axis=2, concat_axis=0, tiled=True)  8.98 us
    all_to_all x2, starting transfers between devices, surface_flux(): lax.all_to_all(mapped, 'deg', split_axis=2, concat_axis=0, tiled=True)  7.44 us
    all_to_all x2, starting transfers between devices, surface_flux(): lax.all_to_all(coeff.astype(jnp.bfloat16), 'deg', split_axis=0, concat_ax...  6.94 us
    unnamed x81, local copies, waits for them, and re-layouts  6.64 us
  transfers between devices with their start and end apart: 14, of which 13 were waited for; matrix products, arithmetic and copies ran while one was open for 7% of the time, Pallas kernels for 0%

commit v1 on v0

--- a/solution.py
+++ b/solution.py
@@ -9,6 +9,22 @@
 time_step = 0.01
 highest = lax.Precision.HIGHEST
 gll_interior = [0.2092992179024789, 0.5917001814331423, 0.8717401485096066]
+
+
+def update_the_scales(xs, join_dim, mat):
+    formed = xs.shape
+    spare = xs.reshape(*formed[:join_dim], mat, formed[join_dim] // mat, *formed[join_dim + 1 :])
+    part_now = jnp.moveaxis(spare, join_dim, 0)
+    return part_now
+
+
+def _name_area(raw, k_dim):
+    raw = jnp.moveaxis(raw, 0, k_dim)
+    local_part = raw.shape
+    plain = raw.reshape(
+        *local_part[:k_dim], local_part[k_dim] * local_part[k_dim + 1], *local_part[k_dim + 2 :]
+    )
+    return plain
 
 
 def padded_2(value, sides, width):
@@ -165,7 +181,16 @@
             coeff.astype(jnp.bfloat16), "deg", split_axis=0, concat_axis=2, tiled=True
         )
         mapped = jnp.einsum("kpq,kcq->kcp", match_ops, owned, preferred_element_type=jnp.float32)
-        matched = lax.all_to_all(mapped, "deg", split_axis=2, concat_axis=0, tiled=True)
+        ready, response = (lax.axis_size("deg"), lax.axis_index("deg"))
+        big = update_the_scales(mapped, 2, ready)
+        pieces_in = [big[response]]
+        for jj in range(1, ready):
+            mixed_arr = big[response ^ jj]
+            pieces_in.append(
+                lax.ppermute(mixed_arr, axis_name="deg", perm=[(c, c ^ jj) for c in range(ready)])
+            )
+        big = jnp.stack(pieces_in, axis=0)[response ^ jnp.arange(ready)]
+        matched = _name_area(big, 0)
         my_waves = lax.dynamic_slice_in_dim(wave_of_slot, tile_index * per_tile, per_tile)
         flat_matched = matched.reshape(per_tile * 2, nb_dev)
         angle = phases(

time: 228 us -> 220 us (0.965)
  other arithmetic: 15.9 us -> 12.3 us
    all_to_all x2 -> x0, waiting for transfers between devices: 8.98 us -> none  [surface_flux(): lax.all_to_all(mapped, 'deg', split_axis=2, concat_axis=0, tiled=True)]
    all_to_all x2 -> x0, starting transfers between devices: 7.44 us -> none  [surface_flux(): lax.all_to_all(mapped, 'deg', split_axis=2, concat_axis=0, tiled=True)]
    ppermute x0 -> x6, starting transfers between devices: none -> 7.08 us  [surface_flux(): lax.ppermute(mixed_arr, axis_name='deg', perm=[(c, c ^ jj) for c in range...]
    ppermute x0 -> x6, waiting for transfers between devices: none -> 5.34 us  [surface_flux(): lax.ppermute(mixed_arr, axis_name='deg', perm=[(c, c ^ jj) for c in range...]
    unnamed x81 -> x80, local copies, waits for them, and re-layouts: 6.64 us -> 3.8 us
    unnamed x2 -> x0, other arithmetic: 2.44 us -> none
  transfers between devices with their start and end apart: 14 -> 18, of which waited for: 13 -> 16; matrix products, arithmetic and copies ran while one was open for 7% -> 7% of each run, Pallas kernels for 0% -> 0%
where the time goes in v1:
time: 220 us; the launch traced here: 219 us
  waiting for transfers between devices  82.7 us (38%)
  blocking collectives  56.3 us (26%)
  starting transfers between devices  20.8 us (9%)
  matrix products  16.8 us (8%)
  between operations  15.3 us (7%)
  local copies, waits for them, and re-layouts  15.2 us (7%)
  other arithmetic  12.3 us (6%)
    unnamed x2, blocking collectives  56.3 us
    reduce_scatter x2, waiting for transfers between devices, surface_flux(): lax.psum_scatter(jnp.dot(table, flat_matched, precision=highest), 'tile',...  54 us
    ppermute x4, waiting for transfers between devices, padded_2(): before = lax.ppermute(last, axis, up)  13.6 us
    dot_general x30, matrix products, apply_along(): return jnp.einsum(formula, blocks, matrix, precision=highest).reshape(shape)  9.27 us
    ppermute x6, starting transfers between devices, surface_flux(): lax.ppermute(mixed_arr, axis_name='deg', perm=[(c, c ^ jj) for c in range...  7.08 us
    all_to_all x2, starting transfers between devices, surface_flux(): lax.all_to_all(coeff.astype(jnp.bfloat16), 'deg', split_axis=0, concat_ax...  6.94 us
    ppermute x4, waiting for transfers between devices, padded_2(): after = lax.ppermute(first, axis, down)  6.38 us
    ppermute x4, starting transfers between devices, padded_2(): after = lax.ppermute(first, axis, down)  5.71 us
  transfers between devices with their start and end apart: 18, of which 16 were waited for; matrix products, arithmetic and copies ran while one was open for 7% of the time, Pallas kernels for 0%

profile of v1, /device:TPU:0, one launch (start us, length us, event | category | flops | bytes accessed | tf_op | source)
XLA Modules:
  0.0 219.3 jit_solution(14381756301650883284)
XLA Ops:
  10.2 1.0 fusion.112
  11.2 30.3 %all-reduce = bf16[32,2,128]{2,0,1:T(8,128)(2,1)S(1)} all-reduce(f32[32,2,128]{2,0,1:T(8,128)S(1)} %fusion.112), channel_id=2, replica_groups=mesh['tile'=8,'deg'=4] {'tile'}, use_global_device_ids=true, to_apply=%region_0.1.clone | all-reduce | flops 8192 | bytes 49152
  41.5 1.2 dynamic-slice.56
  43.9 3.7 %all-to-all-start = ((bf16[4,2,128]{2,1,0:T(2,128)(2,1)}), bf16[4,2,128]{2,1,0:T(2,128)(2,1)S(1)}, u32[]{:S(2)}, u32[]{:S(2)}) async-start(bf16[4,2,128]{2,1,0:T(2,128)(2,1)} %copy.328), calls=%async_computation | async-start | bytes 4096 | tf_op jit(solution)/shard_map/all_to_all | solution.py:180
  49.4 1.1 fusion.47
  50.5 1.0 convolution_bitcast_fusion.6
  51.6 0.9 fusion.176
  53.3 1.0 fusion.50
  62.1 2.9 %collective-permute-start.2 = (f32[1,2,128]{2,1,0:T(2,128)S(1)}, f32[1,2,128]{2,1,0:T(2,128)S(1)}, u32[]{:S(2)}, u32[]{:S(2)}) collective-permute-start(f32[1,2,128]{2,1,0:T(2,128)S(1)} %get-tuple-element.95), channel_id=1, source_target_pairs={{0,3},{1,2},{2,1},{3,0},{4,7},{5,6},{6,5},{7,4},{8,11},{9,10},{10,... | collective-permute-start | bytes 3080 | tf_op jit(solution)/shard_map/ppermute | solution.py:190
  66.6 2.0 collective-permute-done.1
  69.7 0.9 fusion.179
  71.3 26.8 %reduce-scatter.5.cloned.1.call-done = f32[16,128]{1,0:T(8,128)} async-done(((f32[128,128]{1,0:T(8,128)}), f32[16,128]{1,0:T(8,128)}) %reduce-scatter.5.cloned.1.call-update) | async-done | bytes 8208 | tf_op jit(solution)/shard_map/reduce_scatter | solution.py:202
  100.4 3.5 %collective-permute-done.3 = bf16[3,8,1,128]{3,1,2,0:T(8,128)(2,1)S(1)} collective-permute-done((bf16[3,8,1,128]{3,1,2,0:T(8,128)(2,1)S(1)}, bf16[3,8,1,128]{3,1,2,0:T(8,128)(2,1)S(1)}, u32[]{:S(2)}, u32[]{:S(2)}) %collective-permute-start.3) | collective-permute-done | bytes 6176 | tf_op jit(solution)/shard_map/ppermute | solution.py:37
  104.1 2.7 %collective-permute-start.6 = (bf16[3,8,18,1]{3,1,2,0:T(8,128)(2,1)S(1)}, bf16[3,8,18,1]{3,1,2,0:T(8,128)(2,1)S(1)}, u32[]{:S(2)}, u32[]{:S(2)}) collective-permute-start(bf16[3,8,18,1]{3,1,2,0:T(8,128)(2,1)S(1)} %get-tuple-element.73), channel_id=1, source_target_pairs={{1,0},{2,1},{3,2},{0,3},{5,4},{6,5},{7,6},{4,7},{9,8},{10,9},{11,1... | collective-permute-start | bytes 2600 | tf_op jit(solution)/shard_map/ppermute | solution.py:38
  106.8 2.2 %collective-permute-done.6 = bf16[3,8,18,1]{3,1,2,0:T(8,128)(2,1)S(1)} collective-permute-done((bf16[3,8,18,1]{3,1,2,0:T(8,128)(2,1)S(1)}, bf16[3,8,18,1]{3,1,2,0:T(8,128)(2,1)S(1)}, u32[]{:S(2)}, u32[]{:S(2)}) %collective-permute-start.6) | collective-permute-done | bytes 896 | tf_op jit(solution)/shard_map/ppermute | solution.py:38
  109.1 3.3 %collective-permute-done.5 = bf16[3,8,18,1]{3,1,2,0:T(8,128)(2,1)S(1)} collective-permute-done((bf16[3,8,18,1]{3,1,2,0:T(8,128)(2,1)S(1)}, bf16[3,8,18,1]{3,1,2,0:T(8,128)(2,1)S(1)}, u32[]{:S(2)}, u32[]{:S(2)}) %collective-permute-start.5) | collective-permute-done | bytes 896 | tf_op jit(solution)/shard_map/ppermute | solution.py:37
  113.7 1.3 slice.301
  116.0 2.0 maximum_bitcast_fusion
  122.1 26.0 %all-reduce.1 = bf16[32,2,128]{2,0,1:T(8,128)(2,1)S(1)} all-reduce(f32[32,2,128]{2,0,1:T(8,128)S(1)} %fusion.111), channel_id=4, replica_groups=mesh['tile'=8,'deg'=4] {'tile'}, use_global_device_ids=true, to_apply=%region_2.3.clone | all-reduce | flops 8192 | bytes 49152
  148.7 3.2 %all-to-all-start.1 = ((bf16[4,2,128]{2,1,0:T(2,128)(2,1)}), bf16[4,2,128]{2,1,0:T(2,128)(2,1)S(1)}, u32[]{:S(2)}, u32[]{:S(2)}) async-start(bf16[4,2,128]{2,1,0:T(2,128)(2,1)} %copy.379), calls=%async_computation.2 | async-start | bytes 4096 | tf_op jit(solution)/shard_map/all_to_all | solution.py:180
  153.2 3.3 %all-to-all-done.1 = bf16[4,2,128]{2,1,0:T(2,128)(2,1)S(1)} async-done(((bf16[4,2,128]{2,1,0:T(2,128)(2,1)}), bf16[4,2,128]{2,1,0:T(2,128)(2,1)S(1)}, u32[]{:S(2)}, u32[]{:S(2)}) %all-to-all-start.1) | async-done | bytes 2080 | tf_op jit(solution)/shard_map/all_to_all | solution.py:180
  157.3 1.5 collective-permute-start.8
  158.8 1.5 collective-permute-start.7
  161.2 1.1 collective-permute-done.7
  164.1 27.2 %reduce-scatter.7.cloned.1.call-done = f32[16,128]{1,0:T(8,128)} async-done(((f32[128,128]{1,0:T(8,128)}), f32[16,128]{1,0:T(8,128)}) %reduce-scatter.7.cloned.1.call-update) | async-done | bytes 8208 | tf_op jit(solution)/shard_map/reduce_scatter | solution.py:202
  192.7 0.9 collective-permute-done.11
  193.6 3.5 %collective-permute-done.10 = bf16[3,8,1,128]{3,1,2,0:T(8,128)(2,1)S(1)} collective-permute-done((bf16[3,8,1,128]{3,1,2,0:T(8,128)(2,1)S(1)}, bf16[3,8,1,128]{3,1,2,0:T(8,128)(2,1)S(1)}, u32[]{:S(2)}, u32[]{:S(2)}) %collective-permute-start.10) | collective-permute-done | bytes 6176 | tf_op jit(solution)/shard_map/ppermute | solution.py:37
  197.3 2.7 %collective-permute-start.13 = (bf16[3,8,18,1]{3,1,2,0:T(8,128)(2,1)S(1)}, bf16[3,8,18,1]{3,1,2,0:T(8,128)(2,1)S(1)}, u32[]{:S(2)}, u32[]{:S(2)}) collective-permute-start(bf16[3,8,18,1]{3,1,2,0:T(8,128)(2,1)S(1)} %get-tuple-element.71), channel_id=1, source_target_pairs={{1,0},{2,1},{3,2},{0,3},{5,4},{6,5},{7,6},{4,7},{9,8},{10,9},{11,1... | collective-permute-start | bytes 2600 | tf_op jit(solution)/shard_map/ppermute | solution.py:38
  200.0 2.3 %collective-permute-done.13 = bf16[3,8,18,1]{3,1,2,0:T(8,128)(2,1)S(1)} collective-permute-done((bf16[3,8,18,1]{3,1,2,0:T(8,128)(2,1)S(1)}, bf16[3,8,18,1]{3,1,2,0:T(8,128)(2,1)S(1)}, u32[]{:S(2)}, u32[]{:S(2)}) %collective-permute-start.13) | collective-permute-done | bytes 896 | tf_op jit(solution)/shard_map/ppermute | solution.py:38
  202.3 3.3 %collective-permute-done.12 = bf16[3,8,18,1]{3,1,2,0:T(8,128)(2,1)S(1)} collective-permute-done((bf16[3,8,18,1]{3,1,2,0:T(8,128)(2,1)S(1)}, bf16[3,8,18,1]{3,1,2,0:T(8,128)(2,1)S(1)}, u32[]{:S(2)}, u32[]{:S(2)}) %collective-permute-start.12) | collective-permute-done | bytes 896 | tf_op jit(solution)/shard_map/ppermute | solution.py:37
  206.9 1.3 slice.324
  209.2 2.0 maximum_bitcast_fusion.1
  (233 shorter events, 35.9 us)
Async XLA Ops:
  6.5 55.3 %copy-start = (bf16[1,512,512]{2,1,0:T(8,128)(2,1)S(1)}, bf16[1,512,512]{2,1,0:T(8,128)(2,1)}, u32[]{:S(2)}) copy-start(bf16[1,512,512]{2,1,0:T(8,128)(2,1)} %param.13) | copy-start | bytes 1572868
  7.3 90.8 %copy-start.30 = (f32[16]{0:T(128)}, f32[16]{0:T(128)S(1)}, u32[]{:S(2)}) copy-start(f32[16]{0:T(128)S(1)} %mul.669) | copy-start | bytes 196
  8.8 39.7 %copy-start.34 = (f32[16]{0:T(128)}, f32[16]{0:T(128)S(1)}, u32[]{:S(2)}) copy-start(f32[16]{0:T(128)S(1)} %get-tuple-element.103) | copy-start | bytes 196
  43.9 17.9 %all-to-all-start = ((bf16[4,2,128]{2,1,0:T(2,128)(2,1)}), bf16[4,2,128]{2,1,0:T(2,128)(2,1)S(1)}, u32[]{:S(2)}, u32[]{:S(2)}) async-start(bf16[4,2,128]{2,1,0:T(2,128)(2,1)} %copy.328), calls=%async_computation | async-start | bytes 4096 | tf_op jit(solution)/shard_map/all_to_all | solution.py:180
  47.7 50.4 %reduce-scatter.5.cloned.1.call-start = ((), (), s32[]{:S(2)}) async-start(), calls=%async_computation.4 | async-start | bytes 73728 | tf_op jit(solution)/shard_map/reduce_scatter | solution.py:202
  48.5 12.5 %copy-start.24 = (f32[8,2,8]{2,1,0:T(2,128)}, f32[8,2,8]{2,1,0:T(2,128)S(1)}, u32[]{:S(2)}) copy-start(f32[8,2,8]{2,1,0:T(2,128)S(1)} %broadcast_multiply_fusion.3) | copy-start | bytes 1540
  49.4 6.3 %copy-start.2 = (f32[3,8,16,128]{3,2,1,0:T(8,128)S(1)}, f32[3,8,16,128]{3,2,1,0:T(8,128)}, u32[]{:S(2)}) copy-start(f32[3,8,16,128]{3,2,1,0:T(8,128)} %param.12) | copy-start | bytes 589828
  49.4 6.5 %copy-start.1 = (f32[3,8,16,128]{3,2,1,0:T(8,128)S(1)}, f32[3,8,16,128]{3,2,1,0:T(8,128)}, u32[]{:S(2)}) copy-start(f32[3,8,16,128]{3,2,1,0:T(8,128)} %param.11) | copy-start | bytes 589828
  51.6 7.4 %copy-start.10 = (f32[8,16,128]{2,1,0:T(8,128)}, f32[8,16,128]{2,1,0:T(8,128)S(1)}, u32[]{:S(2)}) copy-start(f32[8,16,128]{2,1,0:T(8,128)S(1)} %convolution_bitcast_fusion.6) | copy-start | bytes 196612
  51.6 4.9 %copy-start.22 = (f32[8,8,1,1]{1,0,3,2:T(8,128)S(1)}, f32[8,8,1,1]{1,0,3,2:T(8,128)}, u32[]{:S(2)}) copy-start(f32[8,8,1,1]{1,0,3,2:T(8,128)} %constant.242) | copy-start | bytes 772
  56.5 14.2 %copy-start.6 = (f32[8,16,128]{2,1,0:T(8,128)}, f32[8,16,128]{2,1,0:T(8,128)S(1)}, u32[]{:S(2)}) copy-start(f32[8,16,128]{2,1,0:T(8,128)S(1)} %convolution_bitcast_fusion.9) | copy-start | bytes 196612
  56.7 14.0 %copy-start.12 = (f32[8,16,128]{2,1,0:T(8,128)}, f32[8,16,128]{2,1,0:T(8,128)S(1)}, u32[]{:S(2)}) copy-start(f32[8,16,128]{2,1,0:T(8,128)S(1)} %convolution_bitcast_fusion.10) | copy-start | bytes 196612
  57.5 4.0 %copy-start.8 = (f32[8,16,128]{2,1,0:T(8,128)}, f32[8,16,128]{2,1,0:T(8,128)S(1)}, u32[]{:S(2)}) copy-start(f32[8,16,128]{2,1,0:T(8,128)S(1)} %convolution_bitcast_fusion.13) | copy-start | bytes 196612
  59.7 11.0 %copy-start.18 = (f32[8,16,128]{2,0,1:T(8,128)}, f32[8,16,128]{2,0,1:T(8,128)S(1)}, u32[]{:S(2)}) copy-start(f32[8,16,128]{2,0,1:T(8,128)S(1)} %fusion.80) | copy-start | bytes 196612
  60.2 10.8 %copy-start.20 = (f32[8,16,128]{2,0,1:T(8,128)}, f32[8,16,128]{2,0,1:T(8,128)S(1)}, u32[]{:S(2)}) copy-start(f32[8,16,128]{2,0,1:T(8,128)S(1)} %fusion.86) | copy-start | bytes 196612
  62.1 4.5 %collective-permute-start.2 = (f32[1,2,128]{2,1,0:T(2,128)S(1)}, f32[1,2,128]{2,1,0:T(2,128)S(1)}, u32[]{:S(2)}, u32[]{:S(2)}) collective-permute-start(f32[1,2,128]{2,1,0:T(2,128)S(1)} %get-tuple-element.95), channel_id=1, source_target_pairs={{0,3},{1,2},{2,1},{3,0},{4,7},{5,6},{6,5},{7,4},{8,11},{9,10},{10,... | collective-permute-start | bytes 3080 | tf_op jit(solution)/shard_map/ppermute | solution.py:190
  65.0 3.6 %collective-permute-start.1 = (f32[1,2,128]{2,1,0:T(2,128)S(1)}, f32[1,2,128]{2,1,0:T(2,128)S(1)}, u32[]{:S(2)}, u32[]{:S(2)}) collective-permute-start(f32[1,2,128]{2,1,0:T(2,128)S(1)} %get-tuple-element.96), channel_id=1, source_target_pairs={{0,2},{1,3},{2,0},{3,1},{4,6},{5,7},{6,4},{7,5},{8,10},{9,11},{10,... | collective-permute-start | bytes 3080 | tf_op jit(solution)/shard_map/ppermute | solution.py:190
  65.6 3.6 %collective-permute-start = (f32[1,2,128]{2,1,0:T(2,128)S(1)}, f32[1,2,128]{2,1,0:T(2,128)S(1)}, u32[]{:S(2)}, u32[]{:S(2)}) collective-permute-start(f32[1,2,128]{2,1,0:T(2,128)S(1)} %get-tuple-element.97), channel_id=1, source_target_pairs={{0,1},{1,0},{2,3},{3,2},{4,5},{5,4},{6,7},{7,6},{8,9},{9,8},{10,11... | collective-permute-start | bytes 3080 | tf_op jit(solution)/shard_map/ppermute | solution.py:190
  98.9 1.5 collective-permute-start.4
  99.1 4.9 %collective-permute-start.3 = (bf16[3,8,1,128]{3,1,2,0:T(8,128)(2,1)S(1)}, bf16[3,8,1,128]{3,1,2,0:T(8,128)(2,1)S(1)}, u32[]{:S(2)}, u32[]{:S(2)}) collective-permute-start(bf16[3,8,1,128]{3,1,2,0:T(8,128)(2,1)S(1)} %get-tuple-element.76), channel_id=1, source_target_pairs={{0,4},{4,8},{8,12},{12,16},{16,20},{20,24},{24,28},{28,0},{1,5},{5... | collective-permute-start | bytes 18440 | tf_op jit(solution)/shard_map/ppermute | solution.py:37
  104.1 5.0 %collective-permute-start.6 = (bf16[3,8,18,1]{3,1,2,0:T(8,128)(2,1)S(1)}, bf16[3,8,18,1]{3,1,2,0:T(8,128)(2,1)S(1)}, u32[]{:S(2)}, u32[]{:S(2)}) collective-permute-start(bf16[3,8,18,1]{3,1,2,0:T(8,128)(2,1)S(1)} %get-tuple-element.73), channel_id=1, source_target_pairs={{1,0},{2,1},{3,2},{0,3},{5,4},{6,5},{7,6},{4,7},{9,8},{10,9},{11,1... | collective-permute-start | bytes 2600 | tf_op jit(solution)/shard_map/ppermute | solution.py:38
  106.8 5.6 %collective-permute-start.5 = (bf16[3,8,18,1]{3,1,2,0:T(8,128)(2,1)S(1)}, bf16[3,8,18,1]{3,1,2,0:T(8,128)(2,1)S(1)}, u32[]{:S(2)}, u32[]{:S(2)}) collective-permute-start(bf16[3,8,18,1]{3,1,2,0:T(8,128)(2,1)S(1)} %get-tuple-element.72), channel_id=1, source_target_pairs={{0,1},{1,2},{2,3},{3,0},{4,5},{5,6},{6,7},{7,4},{8,9},{9,10},{10,1... | collective-permute-start | bytes 2600 | tf_op jit(solution)/shard_map/ppermute | solution.py:37
  148.7 7.8 %all-to-all-start.1 = ((bf16[4,2,128]{2,1,0:T(2,128)(2,1)}), bf16[4,2,128]{2,1,0:T(2,128)(2,1)S(1)}, u32[]{:S(2)}, u32[]{:S(2)}) async-start(bf16[4,2,128]{2,1,0:T(2,128)(2,1)} %copy.379), calls=%async_computation.2 | async-start | bytes 4096 | tf_op jit(solution)/shard_map/all_to_all | solution.py:180
  151.9 39.3 %reduce-scatter.7.cloned.1.call-start = ((), (), s32[]{:S(2)}) async-start(), calls=%async_computation.5 | async-start | bytes 73728 | tf_op jit(solution)/shard_map/reduce_scatter | solution.py:202
  152.2 39.1 %copy-start.31 = (f32[16]{0:T(128)S(1)}, f32[16]{0:T(128)}, u32[]{:S(2)}) copy-start(f32[16]{0:T(128)} %copy-done.30) | copy-start | bytes 196
  156.7 4.5 %collective-permute-start.9 = (f32[1,2,128]{2,1,0:T(2,128)S(1)}, f32[1,2,128]{2,1,0:T(2,128)S(1)}, u32[]{:S(2)}, u32[]{:S(2)}) collective-permute-start(f32[1,2,128]{2,1,0:T(2,128)S(1)} %get-tuple-element.91), channel_id=1, source_target_pairs={{0,3},{1,2},{2,1},{3,0},{4,7},{5,6},{6,5},{7,4},{8,11},{9,10},{10,... | collective-permute-start | bytes 3080 | tf_op jit(solution)/shard_map/ppermute | solution.py:190
  157.3 3.9 %collective-permute-start.8 = (f32[1,2,128]{2,1,0:T(2,128)S(1)}, f32[1,2,128]{2,1,0:T(2,128)S(1)}, u32[]{:S(2)}, u32[]{:S(2)}) collective-permute-start(f32[1,2,128]{2,1,0:T(2,128)S(1)} %get-tuple-element.92), channel_id=1, source_target_pairs={{0,2},{1,3},{2,0},{3,1},{4,6},{5,7},{6,4},{7,5},{8,10},{9,11},{10,... | collective-permute-start | bytes 3080 | tf_op jit(solution)/shard_map/ppermute | solution.py:190
  158.8 3.6 %collective-permute-start.7 = (f32[1,2,128]{2,1,0:T(2,128)S(1)}, f32[1,2,128]{2,1,0:T(2,128)S(1)}, u32[]{:S(2)}, u32[]{:S(2)}) collective-permute-start(f32[1,2,128]{2,1,0:T(2,128)S(1)} %get-tuple-element.93), channel_id=1, source_target_pairs={{0,1},{1,0},{2,3},{3,2},{4,5},{5,4},{6,7},{7,6},{8,9},{9,8},{10,11... | collective-permute-start | bytes 3080 | tf_op jit(solution)/shard_map/ppermute | solution.py:190
  192.1 1.5 collective-permute-start.11
  192.3 4.9 %collective-permute-start.10 = (bf16[3,8,1,128]{3,1,2,0:T(8,128)(2,1)S(1)}, bf16[3,8,1,128]{3,1,2,0:T(8,128)(2,1)S(1)}, u32[]{:S(2)}, u32[]{:S(2)}) collective-permute-start(bf16[3,8,1,128]{3,1,2,0:T(8,128)(2,1)S(1)} %get-tuple-element.74), channel_id=1, source_target_pairs={{0,4},{4,8},{8,12},{12,16},{16,20},{20,24},{24,28},{28,0},{1,5},{5... | collective-permute-start | bytes 18440 | tf_op jit(solution)/shard_map/ppermute | solution.py:37
  197.3 5.0 %collective-permute-start.13 = (bf16[3,8,18,1]{3,1,2,0:T(8,128)(2,1)S(1)}, bf16[3,8,18,1]{3,1,2,0:T(8,128)(2,1)S(1)}, u32[]{:S(2)}, u32[]{:S(2)}) collective-permute-start(bf16[3,8,18,1]{3,1,2,0:T(8,128)(2,1)S(1)} %get-tuple-element.71), channel_id=1, source_target_pairs={{1,0},{2,1},{3,2},{0,3},{5,4},{6,5},{7,6},{4,7},{9,8},{10,9},{11,1... | collective-permute-start | bytes 2600 | tf_op jit(solution)/shard_map/ppermute | solution.py:38
  200.0 5.6 %collective-permute-start.12 = (bf16[3,8,18,1]{3,1,2,0:T(8,128)(2,1)S(1)}, bf16[3,8,18,1]{3,1,2,0:T(8,128)(2,1)S(1)}, u32[]{:S(2)}, u32[]{:S(2)}) collective-permute-start(bf16[3,8,18,1]{3,1,2,0:T(8,128)(2,1)S(1)} %get-tuple-element.70), channel_id=1, source_target_pairs={{0,1},{1,2},{2,3},{3,0},{4,5},{5,6},{6,7},{7,4},{8,9},{9,10},{10,1... | collective-permute-start | bytes 2600 | tf_op jit(solution)/shard_map/ppermute | solution.py:37
  (22 other events, 45.6 us)
Sparse Core Ops, SparseCore 0:
  70.8 27.2 reduce-scatter.4
  164.0 27.2 reduce-scatter.6
